TPU v7x, 256 devices: a whole 4x4x8 slice. The times are simulated.
256 devices in a mesh: blk: 64 (over z, x, core), req: 4 (over y).
Axes of the slice: x: 4, y: 4, z: 8, core: 2. Of those that a mesh axis runs over, the one named last changes fastest.
Arguments:
- tokens: bfloat16 [32, 4, 2048], P('req'), may hold values from -6 to 6
- lengths: int32 [32], replicated, may hold values from 1 to 8192, 104857 in all
- slot_request: int32 [32], replicated, may hold values from 0 to 31, each once
- ln1_gain: float32 [2048], replicated, may hold values from 0.5 to 1.5
- ln1_bias: float32 [2048], replicated, may hold values from -3 to 3
- w_query: bfloat16 [2048, 2048], P(None, 'blk'), may hold values from -0.125 to 0.125
- w_key: bfloat16 [2048, 2048], P(None, 'blk'), may hold values from -0.125 to 0.125
- w_value: bfloat16 [2048, 2048], P(None, 'blk'), may hold values from -0.125 to 0.125
- b_query: float32 [2048], P('blk'), may hold values from -3 to 3
- b_key: float32 [2048], P('blk'), may hold values from -3 to 3
- b_value: float32 [2048], P('blk'), may hold values from -3 to 3
- cache_keys: bfloat16 [32, 8192, 2048], P('req', 'blk'), may hold values from -500 to 500
- cache_values: bfloat16 [32, 8192, 2048], P('req', 'blk'), may hold values from -9 to 9
- w_out: bfloat16 [2048, 2048], P(None, 'blk'), may hold values from -0.125 to 0.125
- ln2_gain: float32 [2048], replicated, may hold values from 0.5 to 1.5
- ln2_bias: float32 [2048], replicated, may hold values from -3 to 3
- w_gate: bfloat16 [2048, 5632], P(None, 'blk'), may hold values from -0.125 to 0.125
- w_up: bfloat16 [2048, 5632], P(None, 'blk'), may hold values from -0.125 to 0.125
- w_down: bfloat16 [5632, 2048], P('blk'), may hold values from -0.078125 to 0.078125
Outputs:
- layer_out: bfloat16 [32, 4, 2048], P('req', None, 'blk')
- new_keys: bfloat16 [32, 4, 2048], P('req', None, 'blk')
- new_values: bfloat16 [32, 4, 2048], P('req', None, 'blk')
Inputs may be any that keep to these rules, and one draw needn't show every extreme that they name: `lengths`: every request has 1 or more cached tokens; some request has exactly 8192. A permutation of the 32 requests: cache slot i holds request slot_request[i].
All inputs are finite; a program needn't handle non-finite values.
Results may differ from a plain program's by a relative error of at most 0.012.
The roundings to bfloat16 on the way count: a program that leaves them out, or rounds other values in their place, can miss the bound.
Values may be sent and summed in bfloat16 or wider, within the bound.
No kernel may reach another device: no remote copies, remote signals or barrier semaphores. Data moves between devices by JAX's collectives and lax.ppermute only.
A program may use at most 192 MiB of HBM per device.

v0:
```python
import jax
import jax.numpy as jnp
from jax import lax
from jax.sharding import PartitionSpec as P

D = 2048
HEADS = 32
HEAD_DIM = 64
ROT = 16
NEW = 4


def layer_norm(values, norm_gain, norm_bias):
    average = jnp.mean(values, -1, keepdims=True)
    centered = values - average
    variance = jnp.mean(centered * centered, -1, keepdims=True)
    return centered * lax.rsqrt(variance + 1e-05) * norm_gain + norm_bias


def rotate(heads, positions):
    half_rot = ROT // 2
    frequency = 10000.0 ** (-2.0 * jnp.arange(half_rot, dtype=jnp.float32) / ROT)
    angles = positions.astype(jnp.float32)[..., None, None] * frequency
    cosine = jnp.cos(angles)
    sine = jnp.sin(angles)
    leading = heads[..., :half_rot]
    second = heads[..., half_rot:ROT]
    unrotated = heads[..., ROT:]
    return jnp.concatenate(
        [leading * cosine - second * sine, second * cosine + leading * sine, unrotated], -1
    )


def body(
    tokens,
    lengths,
    slot_request,
    ln1_gain,
    ln1_bias,
    w_query,
    w_key,
    w_value,
    b_query,
    b_key,
    b_value,
    cache_keys,
    cache_values,
    w_out,
    ln2_gain,
    ln2_bias,
    w_gate,
    w_up,
    w_down,
):
    group_index = lax.axis_index("req")
    block_index = lax.axis_index("blk")
    count_req = tokens.shape[0]
    block_len = cache_keys.shape[1]
    col_count = w_query.shape[1]
    row_total = count_req * NEW
    column_start = block_index * col_count
    gathered = lax.all_gather(tokens, "req", axis=0, tiled=True)
    owned_slots = lax.dynamic_slice_in_dim(slot_request, group_index * count_req, count_req)
    inputs = jnp.take(gathered, owned_slots, axis=0).astype(jnp.float32)
    span_lengths = jnp.take(lengths, owned_slots)
    token_rows = inputs.reshape(row_total, D)
    normed = layer_norm(token_rows, ln1_gain, ln1_bias).astype(jnp.bfloat16)
    query_cols = (jnp.dot(normed, w_query, preferred_element_type=jnp.float32) + b_query).astype(
        jnp.bfloat16
    )
    key_cols = (jnp.dot(normed, w_key, preferred_element_type=jnp.float32) + b_key).astype(
        jnp.bfloat16
    )
    value_cols = (jnp.dot(normed, w_value, preferred_element_type=jnp.float32) + b_value).astype(
        jnp.bfloat16
    )
    query_raw, key_raw, value_raw = (
        lax.all_gather(query_cols, "blk", axis=1, tiled=True),
        lax.all_gather(key_cols, "blk", axis=1, tiled=True),
        lax.all_gather(value_cols, "blk", axis=1, tiled=True),
    )
    positions = span_lengths[:, None] + jnp.arange(NEW, dtype=jnp.int32)[None, :]
    head_shape = (count_req, NEW, HEADS, HEAD_DIM)
    queries = rotate(query_raw.astype(jnp.float32).reshape(head_shape), positions).astype(
        jnp.bfloat16
    )
    keys_new = rotate(key_raw.astype(jnp.float32).reshape(head_shape), positions).astype(
        jnp.bfloat16
    )
    values_new = value_raw.reshape(head_shape)
    new_keys_out = lax.dynamic_slice_in_dim(
        keys_new.reshape(count_req, NEW, D), column_start, col_count, 2
    )
    new_values_out = lax.dynamic_slice_in_dim(
        value_raw.reshape(count_req, NEW, D), column_start, col_count, 2
    )
    score_scale = HEAD_DIM ** (-0.5)
    key_heads = cache_keys.reshape(count_req, block_len, HEADS, HEAD_DIM)
    value_heads = cache_values.reshape(count_req, block_len, HEADS, HEAD_DIM)
    scores = (
        jnp.einsum("rthd,rphd->rthp", queries, key_heads, preferred_element_type=jnp.float32)
        * score_scale
    )
    places = block_index * block_len + jnp.arange(block_len, dtype=jnp.int32)
    visible = places[None, None, None, :] < span_lengths[:, None, None, None]
    peak_local = jnp.max(jnp.where(visible, scores, -1e30), -1)
    weights = jnp.where(visible, jnp.exp(scores - peak_local[..., None]), 0.0)
    total_local = jnp.sum(weights, -1)
    accum_local = jnp.einsum(
        "rthp,rphd->rthd",
        weights.astype(jnp.bfloat16),
        value_heads,
        preferred_element_type=jnp.float32,
    )
    fresh_scores = (
        jnp.einsum("rthd,rshd->rths", queries, keys_new, preferred_element_type=jnp.float32)
        * score_scale
    )
    causal = jnp.arange(NEW)[:, None, None] >= jnp.arange(NEW)[None, None, :]
    fresh_peak = jnp.max(jnp.where(causal, fresh_scores, -1e30), -1)
    fresh_weights = jnp.where(causal, jnp.exp(fresh_scores - fresh_peak[..., None]), 0.0)
    fresh_total = jnp.sum(fresh_weights, -1)
    fresh_accum = jnp.einsum(
        "rths,rshd->rthd",
        fresh_weights.astype(jnp.bfloat16),
        values_new,
        preferred_element_type=jnp.float32,
    )
    cache_peak = lax.pmax(peak_local, "blk")
    peak_all = jnp.maximum(cache_peak, fresh_peak)
    scale_local = jnp.exp(peak_local - peak_all)
    scale_new = jnp.exp(fresh_peak - peak_all)
    total_all, accum_all = lax.psum(
        (total_local * scale_local, accum_local * scale_local[..., None]), "blk"
    )
    numer = accum_all + fresh_accum * scale_new[..., None]
    denom = total_all + fresh_total * scale_new
    attended = (numer / denom[..., None]).astype(jnp.bfloat16).reshape(row_total, D)
    input_cols = lax.dynamic_slice_in_dim(token_rows, column_start, col_count, 1)
    residual = input_cols + jnp.dot(attended, w_out, preferred_element_type=jnp.float32)
    whole_rows = lax.all_gather(residual, "blk", axis=1, tiled=True)
    normed_two = layer_norm(whole_rows, ln2_gain, ln2_bias).astype(jnp.bfloat16)
    gate_proj = jnp.dot(normed_two, w_gate, preferred_element_type=jnp.float32)
    up_proj = jnp.dot(normed_two, w_up, preferred_element_type=jnp.float32)
    hidden = (jax.nn.silu(gate_proj) * up_proj).astype(jnp.bfloat16)
    down_cols = lax.psum_scatter(
        lax.dot_general(
            w_down, hidden, (((0,), (1,)), ((), ())), preferred_element_type=jnp.float32
        ),
        "blk",
        scatter_dimension=0,
        tiled=True,
    )
    layer_rows = (residual + down_cols.T).astype(jnp.bfloat16)
    return (layer_rows.reshape(count_req, NEW, col_count), new_keys_out, new_values_out)


def solution(mesh):
    return jax.shard_map(
        body,
        mesh=mesh,
        in_specs=(
            P("req", None, None),
            P(),
            P(),
            P(),
            P(),
            P(None, "blk"),
            P(None, "blk"),
            P(None, "blk"),
            P("blk"),
            P("blk"),
            P("blk"),
            P("req", "blk", None),
            P("req", "blk", None),
            P(None, "blk"),
            P(),
            P(),
            P(None, "blk"),
            P(None, "blk"),
            P("blk", None),
        ),
        out_specs=(P("req", None, "blk"), P("req", None, "blk"), P("req", None, "blk")),
        check_vma=False,
    )
```

profile of v0, /device:TPU:8, one launch (start us, length us, event | category | flops | bytes accessed | tf_op | source)
XLA Modules:
  0.0 900.7 jit_solution(16838919407700512123)
XLA Ops:
  7.3 0.8 compare_and_fusion
  8.1 13.9 %all_gather.15 = bf16[32,4,2048]{2,1,0:T(4,128)(2,1)S(1)} all-gather(bf16[8,4,2048]{2,1,0:T(4,128)(2,1)} %param.19), channel_id=1, replica_groups=mesh['blk'=64,'req'=4] {'req'}, dimensions={0}, use_global_device_ids=true | all-gather | bytes 655360 | tf_op jit(solution)/shard_map/all_gather | solution.py:62
  22.0 0.7 gather_fusion
  23.5 0.9 add_convert_fusion.2
  24.3 1.1 fusion.7
  25.5 53.3 %all_gather.17 = bf16[32,2048]{0,1:T(8,128)(2,1)S(1)} all-gather(bf16[32,32]{0,1:T(8,128)(2,1)S(1)} %copy.128), channel_id=1, replica_groups=mesh['blk'=64,'req'=4] {'blk'}, dimensions={1}, use_global_device_ids=true | all-gather | bytes 133120 | tf_op jit(solution)/shard_map/all_gather | solution.py:79
  79.8 49.3 %all_gather.16 = bf16[32,2048]{0,1:T(8,128)(2,1)S(1)} all-gather(bf16[32,32]{0,1:T(8,128)(2,1)S(1)} %copy.122), channel_id=1, replica_groups=mesh['blk'=64,'req'=4] {'blk'}, dimensions={1}, use_global_device_ids=true | all-gather | bytes 133120 | tf_op jit(solution)/shard_map/all_gather | solution.py:78
  129.9 0.6 gather_fusion.1
  131.6 0.9 multiply_subtract_fusion
  132.5 1.2 maximum_convert_fusion
  134.7 6.4 copy.126
  141.2 3.5 select_reduce_fusion
  144.6 248.7 %pmax.7 = f32[8,4,32]{1,2,0:T(8,128)S(1)} all-reduce(f32[8,4,32]{1,2,0:T(8,128)S(1)} %get-tuple-element.39), channel_id=1, replica_groups=mesh['blk'=64,'req'=4] {'blk'}, use_global_device_ids=true, to_apply=%region_3.4 | all-reduce | flops 1024 | bytes 8192 | tf_op jit(solution)/shard_map/pmax | solution.py:129
  393.4 0.7 fusion.10
  394.0 6.4 copy.127
  400.5 5.4 fusion
  406.3 246.5 %psum.15 = f32[8,4,32]{1,2,0:T(8,128)S(1)} all-reduce(f32[8,4,32]{1,2,0:T(8,128)S(1)} %get-tuple-element.23), channel_id=1, replica_groups=mesh['blk'=64,'req'=4] {'blk'}, use_global_device_ids=true, to_apply=%region_7.8 | all-reduce | flops 1024 | bytes 8192 | tf_op jit(solution)/shard_map/psum | solution.py:133
  653.3 47.0 %all_gather.18 = bf16[32,2048]{0,1:T(8,128)(2,1)S(1)} all-gather(bf16[32,32]{0,1:T(8,128)(2,1)S(1)} %copy.135), channel_id=1, replica_groups=mesh['blk'=64,'req'=4] {'blk'}, dimensions={1}, use_global_device_ids=true | all-gather | bytes 133120 | tf_op jit(solution)/shard_map/all_gather | solution.py:80
  700.9 1.7 fusion.5
  703.3 50.2 %all_gather.19 = f32[32,2048]{0,1:T(8,128)S(1)} all-gather(f32[32,32]{0,1:T(8,128)S(1)} %copy.142), channel_id=1, replica_groups=mesh['blk'=64,'req'=4] {'blk'}, dimensions={1}, use_global_device_ids=true | all-gather | bytes 266240 | tf_op jit(solution)/shard_map/all_gather | solution.py:141
  755.5 1.3 copy.146
  757.9 0.7 constant_dynamic-slice_fusion
  758.6 133.9 %reduce-scatter.4.cloned.1.call-done = f32[32,32]{1,0:T(8,128)} async-done(((f32[2048,32]{1,0:T(8,128)}), f32[32,32]{1,0:T(8,128)}) %reduce-scatter.4.cloned.1.call-update) | async-done | bytes 4112
  892.5 0.8 copy.147
  (89 shorter events, 10.4 us)
Async XLA Ops:
  7.2 747.8 %copy-start = (bf16[88,2048]{1,0:T(8,128)(2,1)S(1)}, bf16[88,2048]{1,0:T(8,128)(2,1)}, u32[]{:S(2)}) copy-start(bf16[88,2048]{1,0:T(8,128)(2,1)} %param.37) | copy-start | bytes 1081348
  7.2 72.4 %copy-start.4 = (bf16[2048,32]{0,1:T(8,128)(2,1)S(1)}, bf16[2048,32]{0,1:T(8,128)(2,1)}, u32[]{:S(2)}) copy-start(bf16[2048,32]{0,1:T(8,128)(2,1)} %param.24) | copy-start | bytes 393220
  7.2 72.4 %copy-start.9 = (f32[32]{0:T(128)S(1)}, f32[32]{0:T(128)}, u32[]{:S(2)}) copy-start(f32[32]{0:T(128)} %param.27) | copy-start | bytes 388
  7.2 693.7 %all-reduce.2.cloned.1.call-start = ((), (), s32[]{:S(2)}) async-start(), calls=%async_computation.1 | async-start | bytes 1048576 | tf_op jit(solution)/shard_map/psum | solution.py:133
  22.9 107.0 %copy-start.1 = (s32[32]{0:T(128)S(1)}, s32[32]{0:T(128)}, u32[]{:S(2)}) copy-start(s32[32]{0:T(128)} %param.20) | copy-start | bytes 388
  400.5 252.6 %copy-start.5 = (bf16[2048,32]{0,1:T(8,128)(2,1)S(1)}, bf16[2048,32]{0,1:T(8,128)(2,1)}, u32[]{:S(2)}) copy-start(bf16[2048,32]{0,1:T(8,128)(2,1)} %param.26) | copy-start | bytes 393220
  400.5 252.6 %copy-start.10 = (f32[32]{0:T(128)S(1)}, f32[32]{0:T(128)}, u32[]{:S(2)}) copy-start(f32[32]{0:T(128)} %param.29) | copy-start | bytes 388
  405.9 486.6 %reduce-scatter.4.cloned.1.call-start = ((), (), s32[]{:S(2)}) async-start(), calls=%async_computation.2 | async-start | bytes 1064960
  700.6 2.5 copy-start.6
  700.9 53.2 %copy-start.7 = (f32[2048]{0:T(1024)S(1)}, f32[2048]{0:T(1024)}, u32[]{:S(2)}) copy-start(f32[2048]{0:T(1024)} %param.34) | copy-start | bytes 24580
  700.9 53.2 %copy-start.8 = (f32[2048]{0:T(1024)S(1)}, f32[2048]{0:T(1024)}, u32[]{:S(2)}) copy-start(f32[2048]{0:T(1024)} %param.33) | copy-start | bytes 24580
  702.7 52.0 %copy-start.2 = (bf16[2048,88]{0,1:T(8,128)(2,1)S(1)}, bf16[2048,88]{0,1:T(8,128)(2,1)}, u32[]{:S(2)}) copy-start(bf16[2048,88]{0,1:T(8,128)(2,1)} %param.35) | copy-start | bytes 1081348
  702.7 52.3 %copy-start.3 = (bf16[2048,88]{0,1:T(8,128)(2,1)S(1)}, bf16[2048,88]{0,1:T(8,128)(2,1)}, u32[]{:S(2)}) copy-start(bf16[2048,88]{0,1:T(8,128)(2,1)} %param.36) | copy-start | bytes 1081348
Sparse Core Ops, SparseCore 0:
  406.0 177.1 all-reduce.1
  757.0 135.4 reduce-scatter.3
where the time goes:
time: 901 us
  blocking collectives  709 us (79%)
  waiting for transfers between devices  134 us (15%)
  local copies, waits for them, and re-layouts  22 us (2%)
  between operations  14.5 us (2%)
  matrix products  13.3 us (1%)
    pmax x1, blocking collectives, body(): cache_peak = lax.pmax(peak_local, 'blk')  249 us
    psum x1, blocking collectives, body(): lax.psum((total_local * scale_local, accum_local * scale_local[..., None]...  246 us
    unnamed x3, waiting for transfers between devices  134 us
    all_gather x1, blocking collectives, body(): lax.all_gather(key_cols, 'blk', axis=1, tiled=True)  53.3 us
    all_gather x1, blocking collectives, body(): whole_rows = lax.all_gather(residual, 'blk', axis=1, tiled=True)  50.2 us
    all_gather x1, blocking collectives, body(): lax.all_gather(query_cols, 'blk', axis=1, tiled=True)  49.3 us
    all_gather x1, blocking collectives, body(): lax.all_gather(value_cols, 'blk', axis=1, tiled=True)  47 us
  transfers between devices with their start and end apart: 2, of which 1 were waited for; matrix products, arithmetic and copies ran while one was open for 0% of the time, Pallas kernels for 0%

commit v1 on v0

--- a/solution.py
+++ b/solution.py
@@ -75,7 +75,9 @@
         jnp.bfloat16
     )
     query_raw, key_raw, value_raw = (
-        lax.all_gather(query_cols, "blk", axis=1, tiled=True),
+        jnp.concatenate(
+            lax.all_to_all(jnp.stack([query_cols] * lax.axis_size("blk")), "blk", 0, 0), axis=1
+        ),
         lax.all_gather(key_cols, "blk", axis=1, tiled=True),
         lax.all_gather(value_cols, "blk", axis=1, tiled=True),
     )

time: 901 us -> 1040 us (1.15)
  waiting for transfers between devices: 134 us -> 312 us
  blocking collectives: 709 us -> 658 us
  starting transfers between devices: 0.08 us -> 12.2 us
    psum x1, waiting for transfers between devices: 0.02 us -> 177 us  [body(): lax.psum((total_local * scale_local, accum_local * scale_local[..., None]...]
    all_gather x1 -> x0, blocking collectives: 49.3 us -> none  [body(): lax.all_gather(query_cols, 'blk', axis=1, tiled=True)]
    all_to_all x0 -> x1, starting transfers between devices: none -> 11.9 us  [body(): lax.all_to_all(jnp.stack([query_cols] * lax.axis_size('blk')), 'blk', 0, 0)]
  transfers between devices with their start and end apart: 2 -> 3, of which waited for: 1 -> 2; matrix products, arithmetic and copies ran while one was open for 0% -> 2% of each run, Pallas kernels for 0% -> 0%
where the time goes in v1:
time: 1040 us
  blocking collectives  658 us (63%)
  waiting for transfers between devices  312 us (30%)
  local copies, waits for them, and re-layouts  24.1 us (2%)
  between operations  14.4 us (1%)
  matrix products  14.2 us (1%)
  starting transfers between devices  12.2 us (1%)
    pmax x1, blocking collectives, body(): cache_peak = lax.pmax(peak_local, 'blk')  249 us
    psum x1, blocking collectives, body(): lax.psum((total_local * scale_local, accum_local * scale_local[..., None]...  246 us
    psum x1, waiting for transfers between devices, body(): lax.psum((total_local * scale_local, accum_local * scale_local[..., None]...  177 us
    unnamed x3, waiting for transfers between devices  135 us
    all_gather x1, blocking collectives, body(): lax.all_gather(key_cols, 'blk', axis=1, tiled=True)  50.8 us
    all_gather x1, blocking collectives, body(): whole_rows = lax.all_gather(residual, 'blk', axis=1, tiled=True)  48.9 us
    all_gather x1, blocking collectives, body(): lax.all_gather(value_cols, 'blk', axis=1, tiled=True)  48.9 us
  transfers between devices with their start and end apart: 3, of which 2 were waited for; matrix products, arithmetic and copies ran while one was open for 2% of the time, Pallas kernels for 0%

profile of v1, /device:TPU:8, one launch (start us, length us, event | category | flops | bytes accessed | tf_op | source)
XLA Modules:
  0.0 1042.9 jit_solution(448286427181409260)
XLA Ops:
  7.2 0.8 compare_and_fusion
  8.0 13.9 %all_gather.12 = bf16[32,4,2048]{2,1,0:T(4,128)(2,1)S(1)} all-gather(bf16[8,4,2048]{2,1,0:T(4,128)(2,1)} %param.19), channel_id=1, replica_groups=mesh['blk'=64,'req'=4] {'req'}, dimensions={0}, use_global_device_ids=true | all-gather | bytes 655360 | tf_op jit(solution)/shard_map/all_gather | solution.py:62
  23.4 0.9 add_convert_fusion.2
  24.2 1.1 fusion.6
  25.4 1.1 reshape.237
  26.5 11.9 %all-to-all-start = ((bf16[64,2,512]{2,1,0:T(2,128)(2,1)}), bf16[64,2,512]{2,1,0:T(2,128)(2,1)S(1)}, u32[]{:S(2)}, u32[]{:S(2)}) async-start(bf16[64,2,512]{2,1,0:T(2,128)(2,1)} %reshape.237), calls=%async_computation | async-start | bytes 262144 | tf_op jit(solution)/shard_map/all_to_all | solution.py:79
  38.5 1.1 fusion.7
  39.7 50.8 %all_gather.13 = bf16[32,2048]{0,1:T(8,128)(2,1)S(1)} all-gather(bf16[32,32]{0,1:T(8,128)(2,1)S(1)} %copy.124), channel_id=1, replica_groups=mesh['blk'=64,'req'=4] {'blk'}, dimensions={1}, use_global_device_ids=true | all-gather | bytes 133120 | tf_op jit(solution)/shard_map/all_gather | solution.py:81
  92.4 6.4 copy.122
  98.8 6.5 copy.123
  105.6 48.9 %all_gather.14 = bf16[32,2048]{0,1:T(8,128)(2,1)S(1)} all-gather(bf16[32,32]{0,1:T(8,128)(2,1)S(1)} %copy.131), channel_id=1, replica_groups=mesh['blk'=64,'req'=4] {'blk'}, dimensions={1}, use_global_device_ids=true | all-gather | bytes 133120 | tf_op jit(solution)/shard_map/all_gather | solution.py:82
  154.7 1.0 reshape.211
  155.8 0.9 multiply_subtract_fusion
  158.4 1.2 maximum_convert_fusion
  160.7 3.5 select_reduce_fusion
  164.2 248.7 %pmax.7 = f32[8,4,32]{1,2,0:T(8,128)S(1)} all-reduce(f32[8,4,32]{1,2,0:T(8,128)S(1)} %get-tuple-element.39), channel_id=1, replica_groups=mesh['blk'=64,'req'=4] {'blk'}, use_global_device_ids=true, to_apply=%region_3.4 | all-reduce | flops 1024 | bytes 8192 | tf_op jit(solution)/shard_map/pmax | solution.py:131
  413.7 246.3 %psum.15 = f32[8,4,32]{1,2,0:T(8,128)S(1)} all-reduce(f32[8,4,32]{1,2,0:T(8,128)S(1)} %get-tuple-element.23), channel_id=1, replica_groups=mesh['blk'=64,'req'=4] {'blk'}, use_global_device_ids=true, to_apply=%region_7.8 | all-reduce | flops 1024 | bytes 8192 | tf_op jit(solution)/shard_map/psum | solution.py:135
  660.3 5.3 fusion
  665.9 177.4 %all-reduce.2.cloned.1.call-done = f32[8,4,32,64]{3,1,2,0:T(4,128)} async-done(((f32[8,4,32,64]{3,1,2,0:T(4,128)}), f32[8,4,32,64]{3,1,2,0:T(4,128)}) %all-reduce.2.cloned.1.call-update) | async-done | bytes 262160 | tf_op jit(solution)/shard_map/psum | solution.py:135
  843.3 1.8 fusion.5
  845.7 48.9 %all_gather.15 = f32[32,2048]{0,1:T(8,128)S(1)} all-gather(f32[32,32]{0,1:T(8,128)S(1)} %copy.138), channel_id=1, replica_groups=mesh['blk'=64,'req'=4] {'blk'}, dimensions={1}, use_global_device_ids=true | all-gather | bytes 266240 | tf_op jit(solution)/shard_map/all_gather | solution.py:143
  896.6 1.3 copy.142
  899.8 134.9 %reduce-scatter.4.cloned.1.call-done = f32[32,32]{1,0:T(8,128)} async-done(((f32[2048,32]{1,0:T(8,128)}), f32[32,32]{1,0:T(8,128)}) %reduce-scatter.4.cloned.1.call-update) | async-done | bytes 4112
  1034.7 0.8 copy.143
  (90 shorter events, 13.1 us)
Async XLA Ops:
  7.2 889.0 %copy-start = (bf16[88,2048]{1,0:T(8,128)(2,1)S(1)}, bf16[88,2048]{1,0:T(8,128)(2,1)}, u32[]{:S(2)}) copy-start(bf16[88,2048]{1,0:T(8,128)(2,1)} %param.37) | copy-start | bytes 1081348
  21.9 69.5 %copy-start.1 = (s32[32]{0:T(128)S(1)}, s32[32]{0:T(128)}, u32[]{:S(2)}) copy-start(s32[32]{0:T(128)} %param.20) | copy-start | bytes 388
  26.5 130.2 %all-to-all-start = ((bf16[64,2,512]{2,1,0:T(2,128)(2,1)}), bf16[64,2,512]{2,1,0:T(2,128)(2,1)S(1)}, u32[]{:S(2)}, u32[]{:S(2)}) async-start(bf16[64,2,512]{2,1,0:T(2,128)(2,1)} %reshape.237), calls=%async_computation | async-start | bytes 262144 | tf_op jit(solution)/shard_map/all_to_all | solution.py:79
  38.4 804.9 %all-reduce.2.cloned.1.call-start = ((), (), s32[]{:S(2)}) async-start(), calls=%async_computation.2 | async-start | bytes 1048576 | tf_op jit(solution)/shard_map/psum | solution.py:135
  98.8 6.5 copy-start.5
  98.8 6.5 copy-start.9
  413.6 429.7 %copy-start.4 = (bf16[8,4,32,64]{3,2,1,0:T(8,128)(2,1)S(1)}, bf16[8,4,32,64]{3,2,1,0:T(8,128)(2,1)}, u32[]{:S(2)}) copy-start(bf16[8,4,32,64]{3,2,1,0:T(8,128)(2,1)} %reshape.211) | copy-start | bytes 393220
  665.6 179.8 %copy-start.6 = (bf16[2048,32]{0,1:T(8,128)(2,1)S(1)}, bf16[2048,32]{0,1:T(8,128)(2,1)}, u32[]{:S(2)}) copy-start(bf16[2048,32]{0,1:T(8,128)(2,1)} %param.32) | copy-start | bytes 393220
  665.6 369.1 %reduce-scatter.4.cloned.1.call-start = ((), (), s32[]{:S(2)}) async-start(), calls=%async_computation.3 | async-start | bytes 1064960
  843.3 51.9 %copy-start.7 = (f32[2048]{0:T(1024)S(1)}, f32[2048]{0:T(1024)}, u32[]{:S(2)}) copy-start(f32[2048]{0:T(1024)} %param.34) | copy-start | bytes 24580
  843.3 51.9 %copy-start.8 = (f32[2048]{0:T(1024)S(1)}, f32[2048]{0:T(1024)}, u32[]{:S(2)}) copy-start(f32[2048]{0:T(1024)} %param.33) | copy-start | bytes 24580
  845.1 50.8 %copy-start.2 = (bf16[2048,88]{0,1:T(8,128)(2,1)S(1)}, bf16[2048,88]{0,1:T(8,128)(2,1)}, u32[]{:S(2)}) copy-start(bf16[2048,88]{0,1:T(8,128)(2,1)} %param.35) | copy-start | bytes 1081348
  845.1 51.0 %copy-start.3 = (bf16[2048,88]{0,1:T(8,128)(2,1)S(1)}, bf16[2048,88]{0,1:T(8,128)(2,1)}, u32[]{:S(2)}) copy-start(bf16[2048,88]{0,1:T(8,128)(2,1)} %param.36) | copy-start | bytes 1081348
Sparse Core Ops, SparseCore 0:
  665.7 177.5 all-reduce.1
  898.1 136.5 reduce-scatter.3
